TPU v7x, 32 devices: a whole 2x2x4 slice. The times are simulated.
32 devices in a mesh: dp: 16 (over z, y, x), lat: 2 (over core).
Axes of the slice: x: 2, y: 2, z: 4, core: 2. Of those that a mesh axis runs over, the one named last changes fastest.
Arguments:
- acts: bfloat16 [2048, 8192], P('dp', 'lat'), may hold values from -6 to 6
- owner_ids: int32 [2048, 4], P('dp'), may hold values from 0 to 31, all different within a row; in each aligned block of 128 rows (0 to 127, 128 to 255, ...) at most 32 rows name the same one
- block_codes: int32 [2048, 4], P('dp'), may hold values from 1 to 3
- weights: bfloat16 [4096, 8192], P(('dp', 'lat')), may hold values from -0.25 to 0.25
- enc_bias: float32 [4096], P(('dp', 'lat')), may hold values from -3 to 3
- dec_bias: float32 [8192], P('lat'), may hold values from -3 to 3
Outputs:
- recon: bfloat16 [2048, 8192], P('dp', 'lat')
- grad_weights: bfloat16 [4096, 8192], P(('dp', 'lat'))
- grad_enc_bias: float32 [4096], P(('dp', 'lat'))
- grad_dec_bias: float32 [8192], P('lat')
Inputs may be any that keep to these rules, and one draw needn't show every extreme that they name: `owner_ids`: each row names 4 different devices; in each aligned block of 128 rows (the rows of one index of dp) no device is named by more than 32 rows, and some device is named by exactly 32. `block_codes`: bit j (j < 2) of an entry says whether block j of that device's 2 blocks is active for the token.
All inputs are finite; a program needn't handle non-finite values.
Results may differ from a plain program's by a relative error of at most 0.0056.
Values may be sent and summed in bfloat16 or wider, within the bound.
No kernel may reach another device: no remote copies, remote signals or barrier semaphores. Data moves between devices by JAX's collectives and lax.ppermute only.
A program may use at most 192 MiB of HBM per device.

v0:
```python
import jax
import jax.numpy as jnp
from jax import lax
from jax.sharding import PartitionSpec as P

BLK_DEV = 2


def owner_work(rows, gate, weights, enc_bias, block_width):
    pre = (
        lax.dot_general(rows, weights, (((1,), (1,)), ((), ())), preferred_element_type=jnp.float32)
        + enc_bias[None, :]
    )
    gate_lat = jnp.repeat(gate.astype(jnp.float32), block_width, axis=1)
    codes = (jnp.maximum(pre, 0.0) * gate_lat).astype(jnp.bfloat16)
    parts = jnp.dot(codes, weights, preferred_element_type=jnp.float32).astype(jnp.bfloat16)
    return (pre, gate_lat, codes, parts)


def owner_grads(rows, errors, weights, pre, gate_lat, codes):
    gcodes = lax.dot_general(
        errors, weights, (((1,), (1,)), ((), ())), preferred_element_type=jnp.float32
    )
    gpre = gcodes * gate_lat * (pre > 0.0).astype(jnp.float32)
    grad_w = lax.dot_general(
        codes, errors, (((0,), (0,)), ((), ())), preferred_element_type=jnp.float32
    )
    grad_w = grad_w + lax.dot_general(
        gpre.astype(jnp.bfloat16),
        rows,
        (((0,), (0,)), ((), ())),
        preferred_element_type=jnp.float32,
    )
    return (grad_w.astype(jnp.bfloat16), jnp.sum(gpre, axis=0))


def slot_tables(owner_ids, block_codes, owner_total, slot_cap, blk_count):
    tok_rows, own_count = owner_ids.shape
    onehot = (
        owner_ids[:, :, None] == jnp.arange(owner_total, dtype=jnp.int32)[None, None, :]
    ).astype(jnp.float32)
    present = jnp.sum(onehot, axis=1)
    lower = (jnp.arange(tok_rows)[None, :] < jnp.arange(tok_rows)[:, None]).astype(jnp.float32)
    before = jnp.dot(lower, present, precision=lax.Precision.HIGHEST)
    slot_of = jnp.sum(onehot * before[:, None, :], axis=2)
    slot_hit = (
        slot_of[:, :, None] == jnp.arange(slot_cap, dtype=jnp.float32)[None, None, :]
    ).astype(jnp.float32)
    select = (onehot[:, :, :, None] * slot_hit[:, :, None, :]).reshape(
        tok_rows, own_count, owner_total * slot_cap
    )
    place = jnp.sum(select, axis=1)
    bits = jnp.stack([block_codes // 2**j % 2 for j in range(blk_count)], axis=-1).astype(
        jnp.float32
    )
    gates = jnp.einsum("tks,tkj->sj", select, bits)
    return (place, gates)


def local(acts, owner_ids, block_codes, weights, enc_bias, dec_bias):
    dp_count = lax.axis_size("dp")
    lat_count = lax.axis_size("lat")
    owner_total = dp_count * lat_count
    tok_rows, own_count = owner_ids.shape
    full_width = weights.shape[1]
    blk_count = BLK_DEV
    block_width = weights.shape[0] // blk_count
    slot_cap = max(2, 2 * tok_rows * own_count // owner_total)
    place, gates = slot_tables(owner_ids, block_codes, owner_total, slot_cap, blk_count)
    lat_hit = (jnp.arange(lat_count, dtype=jnp.int32) == lax.axis_index("lat")).astype(jnp.float32)
    mine = jnp.einsum(
        "tdlc,l->tdc", place.reshape(tok_rows, dp_count, lat_count, slot_cap), lat_hit
    )
    mine_b = mine.reshape(tok_rows, dp_count * slot_cap).astype(jnp.bfloat16)
    mine_gate = jnp.einsum(
        "dlcj,l->dcj", gates.reshape(dp_count, lat_count, slot_cap, blk_count), lat_hit
    )
    whole = lax.all_gather(acts, "lat", axis=1, tiled=True)
    sent = lax.dot_general(
        mine_b, whole, (((0,), (0,)), ((), ())), preferred_element_type=jnp.float32
    )
    sent = sent.astype(jnp.bfloat16).reshape(dp_count, slot_cap, full_width)
    got_rows, got_gate = (
        lax.all_to_all(sent, "dp", split_axis=0, concat_axis=0, tiled=True),
        lax.all_to_all(
            mine_gate.astype(jnp.bfloat16), "dp", split_axis=0, concat_axis=0, tiled=True
        ),
    )
    rows = got_rows.reshape(dp_count * slot_cap, full_width)
    gate = got_gate.reshape(dp_count * slot_cap, blk_count)
    pre, gate_lat, codes, parts = owner_work(rows, gate, weights, enc_bias, block_width)
    back = lax.all_to_all(
        parts.reshape(dp_count, slot_cap, full_width), "dp", split_axis=0, concat_axis=0, tiled=True
    )
    partial_value = jnp.dot(
        mine_b, back.reshape(dp_count * slot_cap, full_width), preferred_element_type=jnp.float32
    )
    summed = lax.psum_scatter(partial_value, "lat", scatter_dimension=1, tiled=True)
    full = dec_bias[None, :] + summed
    err = full - acts.astype(jnp.float32)
    gerr = err.astype(jnp.bfloat16)
    err_whole = lax.all_gather(gerr, "lat", axis=1, tiled=True)
    err_sent = lax.dot_general(
        mine_b, err_whole, (((0,), (0,)), ((), ())), preferred_element_type=jnp.float32
    )
    err_sent = err_sent.astype(jnp.bfloat16).reshape(dp_count, slot_cap, full_width)
    got_err = lax.all_to_all(err_sent, "dp", split_axis=0, concat_axis=0, tiled=True)
    errors = got_err.reshape(dp_count * slot_cap, full_width)
    recon = full.astype(jnp.bfloat16)
    grad_weights, grad_enc_bias = owner_grads(rows, errors, weights, pre, gate_lat, codes)
    grad_dec_bias = lax.psum(jnp.sum(err, axis=0), "dp")
    return (recon, grad_weights, grad_enc_bias, grad_dec_bias)


def solution(mesh):
    in_specs = (
        P("dp", "lat"),
        P("dp", None),
        P("dp", None),
        P(("dp", "lat"), None),
        P(("dp", "lat")),
        P("lat"),
    )
    out_specs = (P("dp", "lat"), P(("dp", "lat"), None), P(("dp", "lat")), P("lat"))
    return jax.shard_map(local, mesh=mesh, in_specs=in_specs, out_specs=out_specs, check_vma=False)
```

profile of v0, /device:TPU:0, one launch (start us, length us, event | category | flops | bytes accessed | tf_op | source)
XLA Modules:
  0.0 737.8 jit_solution(16515403187644802783)
XLA Ops:
  7.2 0.7 all-gather.3.cloned.1.call-update
  7.9 0.7 fusion.37
  8.6 0.7 add_select_fusion.2
  9.4 0.8 fusion.16
  10.2 0.7 fusion.12
  11.1 0.8 fusion.6
  12.7 8.3 %all-to-all-start.1 = ((bf16[16,32,2]{1,2,0:T(2,128)(2,1)}), bf16[16,32,2]{1,2,0:T(2,128)(2,1)S(1)}, u32[]{:S(2)}, u32[]{:S(2)}) async-start(bf16[16,32,2]{1,2,0:T(2,128)(2,1)} %convert_element_type.64), calls=%async_computation.1 | async-start | bytes 16384 | tf_op jit(solution)/shard_map/all_to_all | solution.py:85
  21.8 1.1 all-gather.3.cloned.1.call-done
  22.9 7.2 convolution_convert_fusion.2
  30.1 7.0 all-to-all-start
  37.3 158.9 %all-to-all-done = bf16[16,32,8192]{2,1,0:T(8,128)(2,1)} async-done(((bf16[16,32,8192]{2,1,0:T(8,128)(2,1)}), bf16[16,32,8192]{2,1,0:T(8,128)(2,1)}, u32[]{:S(2)}, u32[]{:S(2)}) %all-to-all-start) | async-done | bytes 8388640 | tf_op jit(solution)/shard_map/all_to_all | solution.py:84
  196.3 6.5 multiply_convert_fusion
  202.7 2.3 convolution_convert_fusion.1
  205.1 220.9 %all_to_all.20 = bf16[16,32,8192]{2,1,0:T(8,128)(2,1)S(1)} all-to-all(bf16[16,32,8192]{2,1,0:T(8,128)(2,1)S(1)} %bitcast.62), channel_id=1, replica_groups=mesh['dp'=16,'lat'=2] {'dp'}, dimensions={0} | all-to-all | bytes 16777216 | tf_op jit(solution)/shard_map/all_to_all | solution.py:92
  426.0 3.2 fusion.63
  429.5 10.7 %reduce-scatter.2.cloned.1.call-done = f32[128,4096]{1,0:T(8,128)} async-done(((f32[128,8192]{1,0:T(8,128)}), f32[128,4096]{1,0:T(8,128)}) %reduce-scatter.2.cloned.1.call-update) | async-done | bytes 2097168 | tf_op jit(solution)/shard_map/reduce_scatter | solution.py:98
  440.2 3.3 fusion.3
  443.5 12.0 %all-gather.5.cloned.1.call-done = bf16[128,8192]{1,0:T(8,128)(2,1)} async-done(((bf16[128,4096]{1,0:T(8,128)(2,1)}), bf16[128,8192]{1,0:T(8,128)(2,1)}) %all-gather.5.cloned.1.call-update) | async-done | bytes 2097168 | tf_op jit(solution)/shard_map/all_gather | solution.py:102
  455.5 7.3 convolution_convert_fusion
  462.8 6.8 all-to-all-start.3
  469.7 244.3 %psum.7 = f32[4096]{0:T(1024)} all-reduce(f32[4096]{0:T(1024)S(1)} %get-tuple-element.4), channel_id=1, replica_groups=mesh['dp'=16,'lat'=2] {'dp'}, use_global_device_ids=true, to_apply=%region_6.7 | all-reduce | flops 4096 | bytes 32768 | tf_op jit(solution)/shard_map/psum | solution.py:111
  713.9 4.8 fusion.65
  718.8 6.2 fusion.64
  725.0 6.3 fusion
  (29 shorter events, 2.5 us)
Async XLA Ops:
  7.2 189.1 %copy-start = (bf16[128,8192]{1,0:T(8,128)(2,1)S(1)}, bf16[128,8192]{1,0:T(8,128)(2,1)}, u32[]{:S(2)}) copy-start(bf16[128,8192]{1,0:T(8,128)(2,1)} %param.9) | copy-start | bytes 6291460
  7.2 15.7 %all-gather.3.cloned.1.call-start = ((), (), s32[]{:S(2)}) async-start(), calls=%async_computation.5 | async-start | bytes 3145728 | tf_op jit(solution)/shard_map/all_gather | solution.py:78
  12.7 17.4 %all-to-all-start.1 = ((bf16[16,32,2]{1,2,0:T(2,128)(2,1)}), bf16[16,32,2]{1,2,0:T(2,128)(2,1)S(1)}, u32[]{:S(2)}, u32[]{:S(2)}) async-start(bf16[16,32,2]{1,2,0:T(2,128)(2,1)} %convert_element_type.64), calls=%async_computation.1 | async-start | bytes 16384 | tf_op jit(solution)/shard_map/all_to_all | solution.py:85
  21.8 404.2 %copy-start.2 = (bf16[1,128,512]{2,0,1:T(2,128)(2,1)}, bf16[1,128,512]{2,0,1:T(2,128)(2,1)S(1)}, u32[]{:S(2)}) copy-start(bf16[1,128,512]{2,0,1:T(2,128)(2,1)S(1)} %fusion.45) | copy-start | bytes 393220
  30.1 166.2 %copy-start.4 = (f32[128]{0:T(128)S(1)}, f32[128]{0:T(128)}, u32[]{:S(2)}) copy-start(f32[128]{0:T(128)} %param.10) | copy-start | bytes 1540
  30.1 166.2 %all-to-all-start = ((bf16[16,32,8192]{2,1,0:T(8,128)(2,1)}), bf16[16,32,8192]{2,1,0:T(8,128)(2,1)}, u32[]{:S(2)}, u32[]{:S(2)}) async-start(bf16[16,32,8192]{2,1,0:T(8,128)(2,1)} %bitcast.59), calls=%async_computation | async-start | bytes 16777216 | tf_op jit(solution)/shard_map/all_to_all | solution.py:84
  37.0 403.1 %reduce-scatter.2.cloned.1.call-start = ((), (), s32[]{:S(2)}) async-start(), calls=%async_computation.6 | async-start | bytes 6291456 | tf_op jit(solution)/shard_map/reduce_scatter | solution.py:98
  429.2 10.9 %copy-start.1 = (bf16[128,4096]{1,0:T(8,128)(2,1)S(1)}, bf16[128,4096]{1,0:T(8,128)(2,1)}, u32[]{:S(2)}) copy-start(bf16[128,4096]{1,0:T(8,128)(2,1)} %param.6) | copy-start | bytes 3145732
  429.2 26.3 %all-gather.5.cloned.1.call-start = ((), (), s32[]{:S(2)}) async-start(), calls=%async_computation.7 | async-start | bytes 3145728 | tf_op jit(solution)/shard_map/all_gather | solution.py:102
  462.8 251.1 %all-to-all-start.3 = ((bf16[16,32,8192]{2,1,0:T(8,128)(2,1)}), bf16[16,32,8192]{2,1,0:T(8,128)(2,1)}, u32[]{:S(2)}, u32[]{:S(2)}) async-start(bf16[16,32,8192]{2,1,0:T(8,128)(2,1)} %bitcast.60), calls=%async_computation.4 | async-start | bytes 16777216 | tf_op jit(solution)/shard_map/all_to_all | solution.py:107
  713.9 4.8 copy-start.3
Sparse Core Ops, SparseCore 0:
  9.6 13.2 all-gather.2
  429.4 10.7 reduce-scatter.1
  443.6 11.8 all-gather.4
where the time goes:
time: 739 us; the launch traced here: 738 us
  blocking collectives  465 us (63%)
  waiting for transfers between devices  183 us (25%)
  matrix products  45.3 us (6%)
  starting transfers between devices  22.4 us (3%)
  between operations  13.9 us (2%)
    psum x1, blocking collectives, local(): grad_dec_bias = lax.psum(jnp.sum(err, axis=0), 'dp')  244 us
    all_to_all x1, blocking collectives, local(): lax.all_to_all(parts.reshape(dp_count, slot_cap, full_width), 'dp', split...  221 us
    all_to_all x1, waiting for transfers between devices, local(): lax.all_to_all(sent, 'dp', split_axis=0, concat_axis=0, tiled=True)  159 us
  transfers between devices with their start and end apart: 6, of which 4 were waited for; matrix products, arithmetic and copies ran while one was open for 2% of the time, Pallas kernels for 0%

commit v1 on v0

--- a/solution.py
+++ b/solution.py
@@ -2,8 +2,10 @@
 import jax.numpy as jnp
 from jax import lax
 from jax.sharding import PartitionSpec as P
+from jax.lax import all_gather
 
 BLK_DEV = 2
+loops_extend = lambda content, comm_axis: jnp.sum(all_gather(content, comm_axis), axis=0)
 
 
 def owner_work(rows, gate, weights, enc_bias, block_width):
@@ -108,7 +110,7 @@
     errors = got_err.reshape(dp_count * slot_cap, full_width)
     recon = full.astype(jnp.bfloat16)
     grad_weights, grad_enc_bias = owner_grads(rows, errors, weights, pre, gate_lat, codes)
-    grad_dec_bias = lax.psum(jnp.sum(err, axis=0), "dp")
+    grad_dec_bias = loops_extend(jnp.sum(err, axis=0), "dp")
     return (recon, grad_weights, grad_enc_bias, grad_dec_bias)
 
 

time: 739 us -> 709 us (0.959); the launches traced: 738 us -> 697 us
  blocking collectives: 465 us -> 423 us
    psum x1 -> x0, blocking collectives: 244 us -> none  [local(): grad_dec_bias = lax.psum(jnp.sum(err, axis=0), 'dp')]
    all_gather x0 -> x1, blocking collectives: none -> 202 us  [all_gather(content, comm_axis)]
where the time goes in v1:
time: 709 us; the launch traced here: 697 us
  blocking collectives  423 us (60%)
  waiting for transfers between devices  183 us (26%)
  matrix products  45.3 us (6%)
  starting transfers between devices  22.4 us (3%)
  between operations  13.9 us (2%)
  other arithmetic  7.82 us (1%)
    all_to_all x1, blocking collectives, local(): lax.all_to_all(parts.reshape(dp_count, slot_cap, full_width), 'dp', split...  221 us
    all_gather x1, blocking collectives, all_gather(content, comm_axis)  202 us
    all_to_all x1, waiting for transfers between devices, local(): lax.all_to_all(sent, 'dp', split_axis=0, concat_axis=0, tiled=True)  159 us
  transfers between devices with their start and end apart: 6, of which 4 were waited for; matrix products, arithmetic and copies ran while one was open for 2% of the time, Pallas kernels for 0%

profile of v1, /device:TPU:0, one launch (start us, length us, event | category | flops | bytes accessed | tf_op | source)
XLA Modules:
  0.0 696.6 jit_solution(7459261461438892784)
XLA Ops:
  7.2 0.7 all-gather.4.cloned.1.call-update
  7.9 0.7 fusion.32
  8.6 0.7 add_select_fusion.2
  9.4 0.8 fusion.11
  10.2 0.7 fusion.7
  11.1 0.8 convolution_bitcast_fusion
  12.7 8.3 %all-to-all-start.1 = ((bf16[16,32,2]{1,2,0:T(2,128)(2,1)}), bf16[16,32,2]{1,2,0:T(2,128)(2,1)S(1)}, u32[]{:S(2)}, u32[]{:S(2)}) async-start(bf16[16,32,2]{1,2,0:T(2,128)(2,1)} %convert_element_type.64), calls=%async_computation.1 | async-start | bytes 16384 | tf_op jit(solution)/shard_map/all_to_all | solution.py:87
  21.8 1.1 all-gather.4.cloned.1.call-done
  22.9 7.2 %convolution_convert_fusion.2 = bf16[512,8192]{1,0:T(8,128)(2,1)} fusion(bf16[128,8192]{1,0:T(8,128)(2,1)} %all-gather.4.cloned.1.call-done, bf16[1,128,512]{2,0,1:T(2,128)(2,1)S(1)} %fusion.40), kind=kOutput, calls=%fused_computation.2 | convolution fusion | flops 1077936128 | bytes 10616832 | tf_op jit(solution)/shard_map/dot_general | solution.py:81
  30.1 7.0 %all-to-all-start = ((bf16[16,32,8192]{2,1,0:T(8,128)(2,1)}), bf16[16,32,8192]{2,1,0:T(8,128)(2,1)}, u32[]{:S(2)}, u32[]{:S(2)}) async-start(bf16[16,32,8192]{2,1,0:T(8,128)(2,1)} %bitcast.60), calls=%async_computation | async-start | bytes 16777216 | tf_op jit(solution)/shard_map/all_to_all | solution.py:86
  37.3 158.9 %all-to-all-done = bf16[16,32,8192]{2,1,0:T(8,128)(2,1)} async-done(((bf16[16,32,8192]{2,1,0:T(8,128)(2,1)}), bf16[16,32,8192]{2,1,0:T(8,128)(2,1)}, u32[]{:S(2)}, u32[]{:S(2)}) %all-to-all-start) | async-done | bytes 8388640 | tf_op jit(solution)/shard_map/all_to_all | solution.py:86
  196.3 6.5 multiply_convert_fusion
  202.7 2.3 convolution_convert_fusion.1
  205.1 220.9 %all_to_all.20 = bf16[16,32,8192]{2,1,0:T(8,128)(2,1)S(1)} all-to-all(bf16[16,32,8192]{2,1,0:T(8,128)(2,1)S(1)} %bitcast.63), channel_id=1, replica_groups=mesh['dp'=16,'lat'=2] {'dp'}, dimensions={0} | all-to-all | bytes 16777216 | tf_op jit(solution)/shard_map/all_to_all | solution.py:94
  426.0 3.2 fusion.58
  429.5 10.7 %reduce-scatter.2.cloned.1.call-done = f32[128,4096]{1,0:T(8,128)} async-done(((f32[128,8192]{1,0:T(8,128)}), f32[128,4096]{1,0:T(8,128)}) %reduce-scatter.2.cloned.1.call-update) | async-done | bytes 2097168 | tf_op jit(solution)/shard_map/reduce_scatter | solution.py:100
  440.2 3.3 fusion.1
  443.5 12.0 %all-gather.6.cloned.1.call-done = bf16[128,8192]{1,0:T(8,128)(2,1)} async-done(((bf16[128,4096]{1,0:T(8,128)(2,1)}), bf16[128,8192]{1,0:T(8,128)(2,1)}) %all-gather.6.cloned.1.call-update) | async-done | bytes 2097168 | tf_op jit(solution)/shard_map/all_gather | solution.py:104
  455.5 7.3 %convolution_convert_fusion = bf16[512,8192]{1,0:T(8,128)(2,1)} fusion(bf16[128,8192]{1,0:T(8,128)(2,1)} %all-gather.6.cloned.1.call-done, bf16[1,128,512]{2,0,1:T(2,128)(2,1)} %copy-done.2), kind=kOutput, calls=%fused_computation | convolution fusion | flops 1077936128 | bytes 10616832 | tf_op jit(solution)/shard_map/dot_general | solution.py:105
  462.8 6.8 all-to-all-start.3
  469.7 202.3 %all-gather = f32[65536]{0:T(1024)S(1)} all-gather(f32[4096]{0:T(1024)S(1)} %get-tuple-element.4), channel_id=2, replica_groups=mesh['dp'=16,'lat'=2] {'dp'}, dimensions={0}, use_global_device_ids=true | all-gather | bytes 278528 | tf_op jit(solution)/shard_map/all_gather | solution.py:8
  672.7 4.8 fusion.60
  677.5 6.2 fusion.59
  683.8 6.3 fusion
  (31 shorter events, 3.2 us)
Async XLA Ops:
  7.2 189.1 %copy-start = (bf16[128,8192]{1,0:T(8,128)(2,1)S(1)}, bf16[128,8192]{1,0:T(8,128)(2,1)}, u32[]{:S(2)}) copy-start(bf16[128,8192]{1,0:T(8,128)(2,1)} %param.9) | copy-start | bytes 6291460
  7.2 15.7 %all-gather.4.cloned.1.call-start = ((), (), s32[]{:S(2)}) async-start(), calls=%async_computation.5 | async-start | bytes 3145728 | tf_op jit(solution)/shard_map/all_gather | solution.py:80
  12.7 17.4 %all-to-all-start.1 = ((bf16[16,32,2]{1,2,0:T(2,128)(2,1)}), bf16[16,32,2]{1,2,0:T(2,128)(2,1)S(1)}, u32[]{:S(2)}, u32[]{:S(2)}) async-start(bf16[16,32,2]{1,2,0:T(2,128)(2,1)} %convert_element_type.64), calls=%async_computation.1 | async-start | bytes 16384 | tf_op jit(solution)/shard_map/all_to_all | solution.py:87
  21.8 404.2 %copy-start.2 = (bf16[1,128,512]{2,0,1:T(2,128)(2,1)}, bf16[1,128,512]{2,0,1:T(2,128)(2,1)S(1)}, u32[]{:S(2)}) copy-start(bf16[1,128,512]{2,0,1:T(2,128)(2,1)S(1)} %fusion.40) | copy-start | bytes 393220
  30.1 166.2 %copy-start.4 = (f32[128]{0:T(128)S(1)}, f32[128]{0:T(128)}, u32[]{:S(2)}) copy-start(f32[128]{0:T(128)} %param.10) | copy-start | bytes 1540
  30.1 166.2 %all-to-all-start = ((bf16[16,32,8192]{2,1,0:T(8,128)(2,1)}), bf16[16,32,8192]{2,1,0:T(8,128)(2,1)}, u32[]{:S(2)}, u32[]{:S(2)}) async-start(bf16[16,32,8192]{2,1,0:T(8,128)(2,1)} %bitcast.60), calls=%async_computation | async-start | bytes 16777216 | tf_op jit(solution)/shard_map/all_to_all | solution.py:86
  37.0 403.1 %reduce-scatter.2.cloned.1.call-start = ((), (), s32[]{:S(2)}) async-start(), calls=%async_computation.6 | async-start | bytes 6291456 | tf_op jit(solution)/shard_map/reduce_scatter | solution.py:100
  429.2 10.9 %copy-start.1 = (bf16[128,4096]{1,0:T(8,128)(2,1)S(1)}, bf16[128,4096]{1,0:T(8,128)(2,1)}, u32[]{:S(2)}) copy-start(bf16[128,4096]{1,0:T(8,128)(2,1)} %param.6) | copy-start | bytes 3145732
  429.2 26.3 %all-gather.6.cloned.1.call-start = ((), (), s32[]{:S(2)}) async-start(), calls=%async_computation.7 | async-start | bytes 3145728 | tf_op jit(solution)/shard_map/all_gather | solution.py:104
  462.8 209.9 %all-to-all-start.3 = ((bf16[16,32,8192]{2,1,0:T(8,128)(2,1)}), bf16[16,32,8192]{2,1,0:T(8,128)(2,1)}, u32[]{:S(2)}, u32[]{:S(2)}) async-start(bf16[16,32,8192]{2,1,0:T(8,128)(2,1)} %bitcast.61), calls=%async_computation.4 | async-start | bytes 16777216 | tf_op jit(solution)/shard_map/all_to_all | solution.py:109
  672.7 4.9 copy-start.3
Sparse Core Ops, SparseCore 0:
  9.6 13.2 all-gather.3
  429.4 10.7 reduce-scatter.1
  443.6 11.8 all-gather.5
